TPU v7x, 256 devices: a whole 4x4x8 slice. The times are simulated.
256 devices in a mesh: scan: 8 (over x, core), mode: 32 (over y, z).
Axes of the slice: x: 4, y: 4, z: 8, core: 2. Of those that a mesh axis runs over, the one named last changes fastest.
Arguments:
- object_field: float32 [2, 2048, 1024], P(None, 'scan'), may hold values from -5 to 5
- probe_modes: float32 [2, 32, 128, 128], P(None, 'mode'), may hold values from -9 to 9
- scan_offsets: int32 [2, 256], P(None, 'scan'), may hold values from 0 to 896, as said below
- measured: float32 [256, 128, 128], P('scan'), may hold values from 0.05 to 3
Outputs:
- object_new: float32 [2, 2048, 1024], P(None, ('scan', 'mode'))
- probe_new: float32 [2, 32, 128, 128], P(None, 'mode')
Inputs may be any that keep to these rules, and one draw needn't show every extreme that they name: scan_offsets[0, j] lies in 0 to 128 and scan_offsets[1, j] in 0 to 896; position j belongs to tile j // 32.
All inputs are finite; a program needn't handle non-finite values.
Results may differ from a plain program's by a relative error of at most 0.0027.
Values sent between devices are 32-bit elements; how exact they have to be, the bound alone decides.
No kernel may reach another device: no remote copies, remote signals or barrier semaphores. Data moves between devices by JAX's collectives and lax.ppermute only.
A program may use at most 128 MiB of HBM per device.

v0:
```python
import math
import jax
import jax.numpy as jnp
from jax import lax
from jax.sharding import PartitionSpec as P

M = 128
NS_ITERS = 8
FLOOR_INTENSITY = 0.1
FLOOR_ILLUM = 1.0
EPSILON = 1e-06


def dft_tables(length):
    pixel_index = jnp.arange(length, dtype=jnp.int32)
    product = pixel_index[:, None] * pixel_index[None, :] % length
    phase_angle = product.astype(jnp.float32) * (2.0 * math.pi / length)
    norm_scale = 1.0 / math.sqrt(length)
    return (
        (jnp.cos(phase_angle) * norm_scale).astype(jnp.bfloat16),
        (-jnp.sin(phase_angle) * norm_scale).astype(jnp.bfloat16),
    )


def right_product(left, table):
    return jnp.einsum("nab,bc->nac", left, table, preferred_element_type=jnp.float32)


def left_product(table, right):
    return jnp.einsum("ab,nbc->nac", table, right, preferred_element_type=jnp.float32)


def forward_pass(wave_re, wave_im, cos_t, sin_t):
    mid_re = (right_product(wave_re, cos_t) - right_product(wave_im, sin_t)).astype(jnp.bfloat16)
    mid_im = (right_product(wave_re, sin_t) + right_product(wave_im, cos_t)).astype(jnp.bfloat16)
    far_re = left_product(cos_t, mid_re) - left_product(sin_t, mid_im)
    far_im = left_product(sin_t, mid_re) + left_product(cos_t, mid_im)
    return (far_re, far_im)


def inverse_pass(spec_re, spec_im, cos_t, sin_t):
    half_re = (right_product(spec_re, cos_t) + right_product(spec_im, sin_t)).astype(jnp.bfloat16)
    half_im = (right_product(spec_im, cos_t) - right_product(spec_re, sin_t)).astype(jnp.bfloat16)
    back_re = left_product(cos_t, half_re) + left_product(sin_t, half_im)
    back_im = left_product(cos_t, half_im) - left_product(sin_t, half_re)
    return (back_re, back_im)


def highest_dot(left, right):
    return jnp.dot(left, right, precision=lax.Precision.HIGHEST, preferred_element_type=jnp.float32)


def gram_of(flat_re, flat_im):
    gram_re = highest_dot(flat_re, flat_re.T) + highest_dot(flat_im, flat_im.T)
    gram_im = highest_dot(flat_re, flat_im.T) - highest_dot(flat_im, flat_re.T)
    return (gram_re, gram_im)


def orthogonal_mix(gram_re, gram_im):
    mode_count = gram_re.shape[0]
    mode_power = jnp.diagonal(gram_re) + EPSILON
    inv_root = 1.0 / jnp.sqrt(mode_power)
    scale_mat = inv_root[:, None] * inv_root[None, :]
    norm_re = gram_re * scale_mat
    norm_im = gram_im * scale_mat
    embedded = jnp.concatenate(
        [jnp.concatenate([norm_re, -norm_im], axis=1), jnp.concatenate([norm_im, norm_re], axis=1)],
        axis=0,
    )
    frobenius = jnp.sqrt(jnp.sum(embedded * embedded))
    identity_mat = jnp.eye(2 * mode_count, dtype=jnp.float32)
    iterate_y = embedded / frobenius
    iterate_z = identity_mat
    for sweep_index in range(NS_ITERS):
        correction = 1.5 * identity_mat - 0.5 * highest_dot(iterate_z, iterate_y)
        iterate_y = highest_dot(iterate_y, correction)
        iterate_z = highest_dot(correction, iterate_z)
    root_inv = iterate_z / jnp.sqrt(frobenius)
    weight_re = root_inv[:mode_count, :mode_count]
    weight_im = root_inv[mode_count:, :mode_count]
    ratio_mat = inv_root[:, None] * jnp.sqrt(mode_power)[None, :]
    return (weight_re * ratio_mat, weight_im * ratio_mat)


def onehot_place(starts, out_len, in_len):
    out_index = jnp.arange(out_len, dtype=jnp.int32)[None, :, None]
    in_index = jnp.arange(in_len, dtype=jnp.int32)[None, None, :]
    return (out_index == starts[:, None, None] + in_index).astype(jnp.bfloat16)


def split_parts(values):
    high = values.astype(jnp.bfloat16)
    rest = values - high.astype(jnp.float32)
    middle = rest.astype(jnp.bfloat16)
    low = (rest - middle.astype(jnp.float32)).astype(jnp.bfloat16)
    return jnp.stack([high, middle, low])


def shards(object_field, probe_modes, scan_offsets, measured):
    mode_index = lax.axis_index("mode")
    cos_t, sin_t = dft_tables(M)
    probe_re = probe_modes[0, 0]
    probe_im = probe_modes[1, 0]
    row_starts = scan_offsets[0]
    col_starts = scan_offsets[1]
    local_count = row_starts.shape[0]
    zero_index = jnp.zeros((), jnp.int32)

    def cut_patch(row_start, col_start):
        return lax.dynamic_slice(object_field, (zero_index, row_start, col_start), (2, M, M))

    obj_patches = jax.vmap(cut_patch)(row_starts, col_starts)
    obj_re = obj_patches[:, 0]
    obj_im = obj_patches[:, 1]
    obj_norm = jnp.sum(obj_re * obj_re + obj_im * obj_im, axis=0)
    wave_re = (probe_re * obj_re - probe_im * obj_im).astype(jnp.bfloat16)
    wave_im = (probe_re * obj_im + probe_im * obj_re).astype(jnp.bfloat16)
    far_re, far_im = forward_pass(wave_re, wave_im, cos_t, sin_t)
    mode_intensity = far_re * far_re + far_im * far_im
    own_light = (probe_re * probe_re + probe_im * probe_im)[None]
    summed = lax.psum(jnp.concatenate([mode_intensity, own_light]), "mode")
    intensity = summed[:local_count]
    light_patch = summed[local_count:]
    amp_ratio = jnp.sqrt(measured / jnp.maximum(intensity, FLOOR_INTENSITY))
    factor = amp_ratio - 1.0
    spec_re = (factor * far_re).astype(jnp.bfloat16)
    spec_im = (factor * far_im).astype(jnp.bfloat16)
    back_re, back_im = inverse_pass(spec_re, spec_im, cos_t, sin_t)
    grad_re = jnp.sum(obj_re * back_re + obj_im * back_im, axis=0)
    grad_im = jnp.sum(obj_re * back_im - obj_im * back_re, axis=0)
    patch_re = probe_re * back_re + probe_im * back_im
    patch_im = probe_re * back_im - probe_im * back_re
    grad_re, grad_im, obj_norm = lax.psum((grad_re, grad_im, obj_norm), "scan")
    step_re = probe_re + grad_re / (obj_norm + EPSILON)
    step_im = probe_im + grad_im / (obj_norm + EPSILON)
    rows_share = object_field.shape[1] // lax.axis_size("mode")
    col_place = onehot_place(col_starts, object_field.shape[2], M)
    row_place = onehot_place(row_starts, object_field.shape[1], M)
    patch_parts = split_parts(jnp.stack([patch_re, patch_im]))
    placed_rows = jnp.einsum(
        "jia,pcjab->pcjib", row_place, patch_parts, preferred_element_type=jnp.float32
    ).astype(jnp.bfloat16)
    grad_tile = jnp.einsum(
        "pcjib,jkb->pcik", placed_rows, col_place, preferred_element_type=jnp.float32
    ).sum(axis=0)
    own_place = onehot_place(row_starts - mode_index * rows_share, rows_share, M)
    light_parts = split_parts(light_patch[0])
    light_rows = jnp.einsum(
        "jia,pab->pjib", own_place, light_parts, preferred_element_type=jnp.float32
    ).astype(jnp.bfloat16)
    light_rows = jnp.einsum(
        "pjib,jkb->pik", light_rows, col_place, preferred_element_type=jnp.float32
    ).sum(axis=0)[None]
    grad_rows = lax.psum_scatter(grad_tile, "mode", scatter_dimension=1, tiled=True)
    own_rows = lax.dynamic_slice_in_dim(object_field, mode_index * rows_share, rows_share, 1)
    object_new = own_rows + grad_rows / jnp.maximum(light_rows, FLOOR_ILLUM)
    flat_mine = jnp.stack([step_re.reshape(-1), step_im.reshape(-1)])[:, None, :]
    every_mode = lax.all_gather(flat_mine, "mode", axis=1, tiled=True)
    gathered_re = every_mode[0]
    gathered_im = every_mode[1]
    gram_re, gram_im = gram_of(gathered_re, gathered_im)
    mix_re, mix_im = orthogonal_mix(gram_re, gram_im)
    column_re = lax.dynamic_slice_in_dim(mix_re, mode_index, 1, 1)
    column_im = lax.dynamic_slice_in_dim(mix_im, mode_index, 1, 1)
    mine_re = highest_dot(column_re.T, gathered_re) - highest_dot(column_im.T, gathered_im)
    mine_im = highest_dot(column_re.T, gathered_im) + highest_dot(column_im.T, gathered_re)
    mine = jnp.stack([mine_re, mine_im])
    probe_new = mine.reshape(2, 1, M, M)
    return (object_new, probe_new)


def solution(mesh):
    placed = (
        P(None, "scan", None),
        P(None, "mode", None, None),
        P(None, "scan"),
        P("scan", None, None),
    )
    return jax.shard_map(
        shards,
        mesh=mesh,
        in_specs=placed,
        out_specs=(P(None, ("scan", "mode"), None), P(None, "mode", None, None)),
        check_vma=False,
    )
```

profile of v0, /device:TPU:2, one launch (start us, length us, event | category | flops | bytes accessed | tf_op | source)
XLA Modules:
  0.0 740.6 jit_solution(13497158749242758823)
XLA Ops:
  9.1 118.7 %while.1 = (s32[]{:T(128)}, f32[2,256,1024]{2,1,0:T(8,128)}, s32[32,3]{0,1:T(4,128)S(1)}, f32[32,2,128,128]{2,3,0,1:T(8,128)}, s32[]{:T(128)}) while((s32[]{:T(128)}, f32[2,256,1024]{2,1,0:T(8,128)}, s32[32,3]{0,1:T(4,128)S(1)}, f32[32,2,128,128]{2,3,0,1:T(8,128)}, s32[]{:T(128)}) %tuple.46), condition=%wide.while_cond, body=%wide.while_body.sunk | while | flops 2 | bytes 786557 | solution.py:110
  9.7 2.3 dynamic-slice_bitcast_fusion.2
  13.4 2.3 dynamic-slice_bitcast_fusion.2
  17.1 2.3 dynamic-slice_bitcast_fusion.2
  20.8 2.3 dynamic-slice_bitcast_fusion.2
  24.5 2.3 dynamic-slice_bitcast_fusion.2
  28.2 2.3 dynamic-slice_bitcast_fusion.2
  31.9 2.3 dynamic-slice_bitcast_fusion.2
  35.6 2.3 dynamic-slice_bitcast_fusion.2
  39.4 2.3 dynamic-slice_bitcast_fusion.2
  43.1 2.3 dynamic-slice_bitcast_fusion.2
  46.7 2.3 dynamic-slice_bitcast_fusion.2
  50.4 2.3 dynamic-slice_bitcast_fusion.2
  54.2 2.3 dynamic-slice_bitcast_fusion.2
  57.9 2.3 dynamic-slice_bitcast_fusion.2
  61.6 2.3 dynamic-slice_bitcast_fusion.2
  65.3 2.3 dynamic-slice_bitcast_fusion.2
  69.0 2.3 dynamic-slice_bitcast_fusion.2
  72.7 2.3 dynamic-slice_bitcast_fusion.2
  76.4 2.3 dynamic-slice_bitcast_fusion.2
  80.1 2.3 dynamic-slice_bitcast_fusion.2
  83.8 2.3 dynamic-slice_bitcast_fusion.2
  87.5 2.3 dynamic-slice_bitcast_fusion.2
  91.2 2.3 dynamic-slice_bitcast_fusion.2
  95.0 2.3 dynamic-slice_bitcast_fusion.2
  98.7 2.3 dynamic-slice_bitcast_fusion.2
  102.4 2.3 dynamic-slice_bitcast_fusion.2
  106.1 2.3 dynamic-slice_bitcast_fusion.2
  109.8 2.3 dynamic-slice_bitcast_fusion.2
  113.5 2.3 dynamic-slice_bitcast_fusion.2
  117.2 2.3 dynamic-slice_bitcast_fusion.2
  124.6 2.3 dynamic-slice_bitcast_fusion.2
  127.8 2.8 fusion.44
  139.5 2.9 copy.40
  142.5 154.0 %all-reduce.4.cloned.1.call-done = f32[33,128,128]{1,2,0:T(8,128)} async-done(((f32[33,128,128]{1,2,0:T(8,128)}), f32[33,128,128]{1,2,0:T(8,128)}) %all-reduce.4.cloned.1.call-update) | async-done | bytes 2162704 | tf_op jit(solution)/shard_map/psum | solution.py:121
  296.5 4.0 fusion.40
  306.8 2.7 fusion.35
  309.9 3.1 fusion.26
  313.6 5.2 fusion.320
  318.8 14.9 %bitcast_reduce_fusion = f32[2,256,1024]{2,1,0:T(8,128)} fusion(s32[32,128]{1,0:T(8,128)S(1)} %get-tuple-element.62, bf16[3,2,32,256,128]{4,3,2,1,0:T(8,128)(2,1)S(1)} %fusion.320), kind=kOutput, calls=%fused_computation.19 | convolution fusion | flops 12890144768 | bytes 14696448 | tf_op jit(solution)/shard_map/pcjib,jkb->pcik/dot_general | solution.py:143
  334.0 40.0 %all-reduce.6.cloned.1.call-done = (f32[128,128]{0,1:T(8,128)}, f32[128,128]{0,1:T(8,128)}, f32[128,128]{0,1:T(8,128)}) async-done(((f32[128,128]{0,1:T(8,128)}, f32[128,128]{0,1:T(8,128)}, f32[128,128]{0,1:T(8,128)}), (f32[128,128]{0,1:T(8,128)}, f32[128,128]{0,1:T(8,128)}, f32[128,128]{0,1:T(8,128)})) %all-reduce.6.cloned.1.call-update) | async-done | bytes 196624 | tf_op jit(solution)/shard_map/psum | solution.py:133
  376.8 3.2 fusion.61
  380.0 217.7 %reduce-scatter.2.cloned.1.call-done = f32[2,8,1024]{2,1,0:T(8,128)} async-done(((f32[2,256,1024]{2,1,0:T(8,128)}), f32[2,8,1024]{2,1,0:T(8,128)}) %reduce-scatter.2.cloned.1.call-update) | async-done | bytes 65552 | tf_op jit(solution)/shard_map/reduce_scatter | solution.py:154
  599.2 81.5 %all-gather.3.cloned.1.call-done = f32[2,524288]{1,0:T(2,128)} async-done(((f32[2,16384]{1,0:T(2,128)}), f32[2,524288]{1,0:T(2,128)}) %all-gather.3.cloned.1.call-update) | async-done | bytes 4194320 | tf_op jit(solution)/shard_map/all_gather | solution.py:158
  680.8 26.1 %slice_reduce_fusion.1 = (f32[524288]{0:T(1024)}, f32[524288]{0:T(1024)}) fusion(f32[2,524288]{1,0:T(2,128)} %all-gather.3.cloned.1.call-done), kind=kLoop, calls=%fused_computation.29 | loop fusion | bytes 8388608 | tf_op jit(solution)/shard_map/slice | solution.py:159
  710.4 3.0 squeeze.26
  713.4 3.5 fusion.223
  719.6 3.4 fusion.219
  (220 shorter events, 84.6 us)
Async XLA Ops:
  7.2 289.3 %all-reduce.4.cloned.1.call-start = ((), (), s32[]{:S(2)}) async-start(), calls=%async_computation.1 | async-start | bytes 4325376 | tf_op jit(solution)/shard_map/psum | solution.py:121
  139.1 234.8 %all-reduce.6.cloned.1.call-start = ((), (), s32[]{:S(2)}) async-start(), calls=%async_computation.4 | async-start | bytes 393216 | tf_op jit(solution)/shard_map/psum | solution.py:133
  139.5 2.9 copy-start.3
  304.6 2.2 copy-start.2
  313.0 284.7 %reduce-scatter.2.cloned.1.call-start = ((), (), s32[]{:S(2)}) async-start(), calls=%async_computation.2 | async-start | bytes 2162688 | tf_op jit(solution)/shard_map/reduce_scatter | solution.py:154
  333.7 347.0 %all-gather.3.cloned.1.call-start = ((), (), s32[]{:S(2)}) async-start(), calls=%async_computation.3 | async-start | bytes 4325376 | tf_op jit(solution)/shard_map/all_gather | solution.py:158
  713.4 3.6 copy-start
  725.2 4.6 copy-start.1
Sparse Core Ops, SparseCore 0:
  139.2 157.2 all-reduce.3
  313.2 60.7 all-reduce.5
  377.8 219.9 reduce-scatter.1
  600.8 79.9 all-gather.2
where the time goes:
time: 751 us; the launch traced here: 741 us
  waiting for transfers between devices  493 us (66%)
  local copies, waits for them, and re-layouts  155 us (21%)
  matrix products  56.6 us (8%)
  other arithmetic  18.5 us (2%)
  between operations  15.2 us (2%)
    reduce_scatter x1, waiting for transfers between devices, shards(): lax.psum_scatter(grad_tile, 'mode', scatter_dimension=1, tiled=True)  218 us
    psum x1, waiting for transfers between devices, shards(): summed = lax.psum(jnp.concatenate([mode_intensity, own_light]), 'mode')  154 us
    gather x160, local copies, waits for them, and re-layouts  118 us
    all_gather x1, waiting for transfers between devices, shards(): every_mode = lax.all_gather(flat_mine, 'mode', axis=1, tiled=True)  81.5 us
    psum x1, waiting for transfers between devices, shards(): grad_re, grad_im, obj_norm = lax.psum((grad_re, grad_im, obj_norm), 'scan')  40 us
    slice x1, local copies, waits for them, and re-layouts, shards(): gathered_re = every_mode[0]  26.1 us
    dot_general x31, matrix products, highest_dot(): jnp.dot(left, right, precision=lax.Precision.HIGHEST, preferred_element_t...  18.8 us
  transfers between devices with their start and end apart: 4, of which 4 were waited for; matrix products, arithmetic and copies ran while one was open for 4% of the time, Pallas kernels for 0%

commit v1 on v0

--- a/solution.py
+++ b/solution.py
@@ -155,7 +155,9 @@
     own_rows = lax.dynamic_slice_in_dim(object_field, mode_index * rows_share, rows_share, 1)
     object_new = own_rows + grad_rows / jnp.maximum(light_rows, FLOOR_ILLUM)
     flat_mine = jnp.stack([step_re.reshape(-1), step_im.reshape(-1)])[:, None, :]
-    every_mode = lax.all_gather(flat_mine, "mode", axis=1, tiled=True)
+    every_mode = jnp.concatenate(
+        lax.all_to_all(jnp.stack([flat_mine] * lax.axis_size("mode")), "mode", 0, 0), axis=1
+    )
     gathered_re = every_mode[0]
     gathered_im = every_mode[1]
     gram_re, gram_im = gram_of(gathered_re, gathered_im)

time: 751 us -> 709 us (0.944)
  waiting for transfers between devices: 493 us -> 448 us
  local copies, waits for them, and re-layouts: 155 us -> 133 us
  matrix products: 56.6 us -> 71.7 us
  starting transfers between devices: 1.15 us -> 10.5 us
    all_gather x1 -> x0, waiting for transfers between devices: 81.5 us -> none  [shards(): every_mode = lax.all_gather(flat_mine, 'mode', axis=1, tiled=True)]
    slice x1, local copies, waits for them, and re-layouts: 26.1 us -> 2.5 us  [shards(): gathered_re = every_mode[0]]
    reduce_scatter x1, waiting for transfers between devices: 218 us -> 236 us  [shards(): lax.psum_scatter(grad_tile, 'mode', scatter_dimension=1, tiled=True)]
    psum x1, waiting for transfers between devices: 40 us -> 57.6 us  [shards(): grad_re, grad_im, obj_norm = lax.psum((grad_re, grad_im, obj_norm), 'scan')]
    all_to_all x0 -> x1, starting transfers between devices: none -> 9.98 us  [shards(): lax.all_to_all(jnp.stack([flat_mine] * lax.axis_size('mode')), 'mode', 0, 0)]
    dot_general x31, matrix products: 18.8 us -> 28.6 us  [highest_dot(): jnp.dot(left, right, precision=lax.Precision.HIGHEST, preferred_element_t...]
  transfers between devices with their start and end apart: 4 -> 4, of which waited for: 4 -> 3; matrix products, arithmetic and copies ran while one was open for 4% -> 6% of each run, Pallas kernels for 0% -> 0%
where the time goes in v1:
time: 709 us; the launch traced here: 700 us
  waiting for transfers between devices  448 us (63%)
  local copies, waits for them, and re-layouts  133 us (19%)
  matrix products  71.7 us (10%)
  other arithmetic  20.5 us (3%)
  between operations  15.2 us (2%)
  starting transfers between devices  10.5 us (1%)
    reduce_scatter x1, waiting for transfers between devices, shards(): lax.psum_scatter(grad_tile, 'mode', scatter_dimension=1, tiled=True)  236 us
    psum x1, waiting for transfers between devices, shards(): summed = lax.psum(jnp.concatenate([mode_intensity, own_light]), 'mode')  154 us
    gather x160, local copies, waits for them, and re-layouts  119 us
    psum x1, waiting for transfers between devices, shards(): grad_re, grad_im, obj_norm = lax.psum((grad_re, grad_im, obj_norm), 'scan')  57.6 us
    dot_general x31, matrix products, highest_dot(): jnp.dot(left, right, precision=lax.Precision.HIGHEST, preferred_element_t...  28.6 us
    dot_general x1, matrix products, shards(): jnp.einsum('pcjib,jkb->pcik', placed_rows, col_place, preferred_element_t...  17.8 us
  transfers between devices with their start and end apart: 4, of which 3 were waited for; matrix products, arithmetic and copies ran while one was open for 6% of the time, Pallas kernels for 0%

profile of v1, /device:TPU:2, one launch (start us, length us, event | category | flops | bytes accessed | tf_op | source)
XLA Modules:
  0.0 699.6 jit_solution(12897498428507521943)
XLA Ops:
  9.1 119.0 %while.1 = (s32[]{:T(128)}, f32[2,256,1024]{2,1,0:T(8,128)}, s32[32,3]{0,1:T(4,128)S(1)}, f32[32,2,128,128]{2,3,0,1:T(8,128)}, s32[]{:T(128)}) while((s32[]{:T(128)}, f32[2,256,1024]{2,1,0:T(8,128)}, s32[32,3]{0,1:T(4,128)S(1)}, f32[32,2,128,128]{2,3,0,1:T(8,128)}, s32[]{:T(128)}) %tuple.46), condition=%wide.while_cond, body=%wide.while_body.sunk | while | flops 2 | bytes 786557 | solution.py:110
  9.7 2.3 dynamic-slice_bitcast_fusion.2
  13.4 2.3 dynamic-slice_bitcast_fusion.2
  17.2 2.3 dynamic-slice_bitcast_fusion.2
  20.9 2.3 dynamic-slice_bitcast_fusion.2
  24.6 2.3 dynamic-slice_bitcast_fusion.2
  28.3 2.3 dynamic-slice_bitcast_fusion.2
  32.1 2.3 dynamic-slice_bitcast_fusion.2
  35.8 2.3 dynamic-slice_bitcast_fusion.2
  39.5 2.3 dynamic-slice_bitcast_fusion.2
  43.2 2.3 dynamic-slice_bitcast_fusion.2
  46.9 2.3 dynamic-slice_bitcast_fusion.2
  50.6 2.3 dynamic-slice_bitcast_fusion.2
  54.4 2.3 dynamic-slice_bitcast_fusion.2
  58.1 2.3 dynamic-slice_bitcast_fusion.2
  65.5 2.3 dynamic-slice_bitcast_fusion.2
  69.2 2.3 dynamic-slice_bitcast_fusion.2
  72.9 2.3 dynamic-slice_bitcast_fusion.2
  76.7 2.3 dynamic-slice_bitcast_fusion.2
  80.4 2.3 dynamic-slice_bitcast_fusion.2
  87.8 2.3 dynamic-slice_bitcast_fusion.2
  91.5 2.3 dynamic-slice_bitcast_fusion.2
  98.9 2.3 dynamic-slice_bitcast_fusion.2
  102.7 2.3 dynamic-slice_bitcast_fusion.2
  106.4 2.3 dynamic-slice_bitcast_fusion.2
  113.8 2.3 dynamic-slice_bitcast_fusion.2
  121.3 2.3 dynamic-slice_bitcast_fusion.2
  125.0 2.3 dynamic-slice_bitcast_fusion.2
  128.1 2.8 fusion.62
  139.6 2.9 copy.40
  142.7 154.2 %all-reduce.4.cloned.1.call-done = f32[33,128,128]{1,2,0:T(8,128)} async-done(((f32[33,128,128]{1,2,0:T(8,128)}), f32[33,128,128]{1,2,0:T(8,128)}) %all-reduce.4.cloned.1.call-update) | async-done | bytes 2162704 | tf_op jit(solution)/shard_map/psum | solution.py:121
  296.9 4.0 fusion.58
  307.2 4.1 fusion.53
  311.3 3.3 fusion.25
  314.6 57.6 %all-reduce.6.cloned.1.call-done = (f32[128,128]{0,1:T(8,128)}, f32[128,128]{0,1:T(8,128)}, f32[128,128]{0,1:T(8,128)}) async-done(((f32[128,128]{0,1:T(8,128)}, f32[128,128]{0,1:T(8,128)}, f32[128,128]{0,1:T(8,128)}), (f32[128,128]{0,1:T(8,128)}, f32[128,128]{0,1:T(8,128)}, f32[128,128]{0,1:T(8,128)})) %all-reduce.6.cloned.1.call-update) | async-done | bytes 196624 | tf_op jit(solution)/shard_map/psum | solution.py:133
  373.4 6.0 stack.42
  379.4 10.0 %all-to-all-start = ((f32[32,2,1,16384]{3,2,1,0:T(1,128)}), f32[32,2,1,16384]{3,2,1,0:T(1,128)}, u32[]{:S(2)}, u32[]{:S(2)}) async-start(f32[32,2,1,16384]{3,2,1,0:T(1,128)} %stack.42), calls=%async_computation.1 | async-start | bytes 8388608 | tf_op jit(solution)/shard_map/all_to_all | solution.py:159
  389.7 2.9 fusion.26
  392.6 6.3 fusion.343
  398.9 17.8 %bitcast_reduce_fusion = f32[2,256,1024]{2,1,0:T(8,128)} fusion(s32[32,128]{1,0:T(8,128)S(1)} %get-tuple-element.62, bf16[3,2,32,256,128]{4,3,2,1,0:T(8,128)(2,1)} %fusion.343), kind=kOutput, calls=%fused_computation.19 | convolution fusion | flops 12890144768 | bytes 14696448 | tf_op jit(solution)/shard_map/pcjib,jkb->pcik/dot_general | solution.py:143
  417.6 3.2 fusion.89
  420.9 236.0 %reduce-scatter.2.cloned.1.call-done = f32[2,8,1024]{2,1,0:T(8,128)} async-done(((f32[2,256,1024]{2,1,0:T(8,128)}), f32[2,8,1024]{2,1,0:T(8,128)}) %reduce-scatter.2.cloned.1.call-update) | async-done | bytes 65552 | tf_op jit(solution)/shard_map/reduce_scatter | solution.py:154
  658.3 2.5 fusion.253
  660.9 2.8 fusion.38
  663.7 4.2 fusion.34
  667.9 3.0 fusion.100
  671.7 5.6 fusion.256
  687.5 2.4 fusion.40
  (220 shorter events, 89.7 us)
Async XLA Ops:
  7.2 289.7 %all-reduce.4.cloned.1.call-start = ((), (), s32[]{:S(2)}) async-start(), calls=%async_computation.2 | async-start | bytes 4325376 | tf_op jit(solution)/shard_map/psum | solution.py:121
  139.4 232.8 %all-reduce.6.cloned.1.call-start = ((), (), s32[]{:S(2)}) async-start(), calls=%async_computation.4 | async-start | bytes 393216 | tf_op jit(solution)/shard_map/psum | solution.py:133
  139.6 2.9 copy-start.4
  305.0 2.2 copy-start.2
  379.4 278.9 %all-to-all-start = ((f32[32,2,1,16384]{3,2,1,0:T(1,128)}), f32[32,2,1,16384]{3,2,1,0:T(1,128)}, u32[]{:S(2)}, u32[]{:S(2)}) async-start(f32[32,2,1,16384]{3,2,1,0:T(1,128)} %stack.42), calls=%async_computation.1 | async-start | bytes 8388608 | tf_op jit(solution)/shard_map/all_to_all | solution.py:159
  389.4 267.4 %reduce-scatter.2.cloned.1.call-start = ((), (), s32[]{:S(2)}) async-start(), calls=%async_computation.3 | async-start | bytes 2162688 | tf_op jit(solution)/shard_map/reduce_scatter | solution.py:154
  389.7 2.9 copy-start.3
  660.8 7.0 %copy-start = (f32[1,32,1,16384]{3,2,0,1:T(1,128)}, f32[1,32,1,16384]{3,2,0,1:T(1,128)S(1)}, u32[]{:S(2)}) copy-start(f32[1,32,1,16384]{3,2,0,1:T(1,128)S(1)} %get-tuple-element.37) | copy-start | bytes 6291460
  678.7 4.2 copy-start.1
Sparse Core Ops, SparseCore 0:
  139.5 157.3 all-reduce.3
  311.4 60.6 all-reduce.5
  416.8 239.9 reduce-scatter.1
